TPU v7x, 256 devices: a whole 4x4x8 slice. The times are simulated.
256 devices in a mesh: prow: 64 (over x, z, core), pcol: 4 (over y).
Axes of the slice: x: 4, y: 4, z: 8, core: 2. Of those that a mesh axis runs over, the one named last changes fastest.
Arguments:
- right_side: float32 [512, 65536], P('pcol', 'prow'), may hold values from -6 to 6
- factor: float32 [65536, 2048], P('prow', 'pcol'), may hold values from -0.125 to 0.125
- inverses: float32 [2048, 512], replicated, as said below
Outputs:
- solved: float32 [512, 65536], P('pcol', 'prow')
Inputs may be any that keep to these rules, and one draw needn't show every extreme that they name: Each 512 x 512 block of inverses is lower triangular with a positive diagonal.
All inputs are finite; a program needn't handle non-finite values.
Results may differ from a plain program's by a relative error of at most 0.0001.
Values sent between devices are 32-bit elements; how exact they have to be, the bound alone decides.
No kernel may reach another device: no remote copies, remote signals or barrier semaphores. Data moves between devices by JAX's collectives and lax.ppermute only.
A program may use at most 64 MiB of HBM per device.

v0:
```python
import jax
import jax.numpy as jnp
from jax import lax
from jax.sharding import PartitionSpec as P


def contract(left, right):
    return lax.dot_general(
        left,
        right,
        (((1,), (1,)), ((), ())),
        precision=lax.Precision.HIGHEST,
        preferred_element_type=jnp.float32,
    )


AXES = ("prow", "pcol")


def per_device(right_side, factor, inverses):
    block = factor.shape[1]
    rhs_width = right_side.shape[0]
    n_col = lax.axis_size("pcol")
    n_row = lax.axis_size("prow")
    steps = n_col
    row_at = lax.axis_index("prow")
    col_at = lax.axis_index("pcol")

    def at(p, c):
        return p * n_col + c

    top_rhs = right_side[:, :block]
    first_rhs = top_rhs
    for i in range(1, steps):
        pairs = [(at(0, c), at(i, c)) for c in range(n_col)]
        first_rhs = jnp.where(row_at == i, lax.ppermute(top_rhs, AXES, pairs), first_rhs)
    first_rhs, first_rows = lax.optimization_barrier((first_rhs, factor[:block]))
    lower_first = lax.all_gather(first_rows, "pcol", axis=1, tiled=True)
    second_rows, _ = lax.optimization_barrier((factor[block:], lower_first))
    lower_second = lax.all_gather(second_rows, "pcol", axis=1, tiled=True)
    acc = jnp.zeros((rhs_width, block), jnp.float32)
    own = jnp.zeros((rhs_width, block), jnp.float32)
    for k in range(steps):
        if k == 0:
            solved = contract(first_rhs, inverses[:block])
        else:
            solved = contract(top_rhs - acc, inverses[k * block : (k + 1) * block])
        own = jnp.where(row_at == k, solved, own)
        if k == steps - 2:
            own_early = own
        if k == steps - 1:
            break
        if k == 0:
            arrived = solved
        else:
            arrived = jnp.zeros_like(solved)
            for i in range(k + 1, steps):
                pairs = [(at(k, c), at(i, c)) for c in range(n_col)]
                arrived = arrived + lax.ppermute(solved, AXES, pairs)
        acc = acc + contract(arrived, lower_first[:, k * block : (k + 1) * block])
    fan_z = min(steps, n_row // steps)
    stride_x = steps * fan_z
    spread = []
    for piece, sources in ((own_early, range(steps - 1)), (own, (steps - 1,))):
        for stride, fan in ((stride_x, n_row // stride_x), (steps, fan_z)):
            holders = [p for p in range(n_row) if p % (stride * fan) in sources]
            received = piece
            for hop in sorted(range(1, fan), key=lambda h: -min(h, fan - h)):
                pairs = [(p, p + hop * stride) for p in holders]
                arrived = lax.ppermute(piece, "prow", pairs)
                received = jnp.where(row_at % (stride * fan) // stride == hop, arrived, received)
            piece = jnp.where(row_at % stride < steps, received, piece)
        spread.append(piece)
    piece = jnp.where(row_at % steps == steps - 1, spread[1], spread[0])
    b0 = row_at % 2
    b1 = row_at // 2 % 2
    other = lax.ppermute(piece, "prow", [(p, p ^ 2) for p in range(n_row)])
    pair = jnp.where(
        b1 == 0, jnp.concatenate([piece, other], axis=1), jnp.concatenate([other, piece], axis=1)
    )
    theirs = lax.ppermute(pair, "prow", [(p, p ^ 1) for p in range(n_row)])
    mine, yours = ((pair[:, :block], pair[:, block:]), (theirs[:, :block], theirs[:, block:]))
    mine_first = jnp.concatenate([mine[0], yours[0], mine[1], yours[1]], axis=1)
    theirs_first = jnp.concatenate([yours[0], mine[0], yours[1], mine[1]], axis=1)
    panel = jnp.where(b0 == 0, mine_first, theirs_first)
    second = right_side[:, block:] - contract(panel, lower_second)
    first = right_side[:, :block] - contract(panel, lower_first)
    head_block = jnp.where(row_at < steps, own, first)
    return jnp.concatenate([head_block, second], axis=1)


def solution(mesh):
    return jax.shard_map(
        per_device,
        mesh=mesh,
        in_specs=(P("pcol", "prow"), P("prow", "pcol"), P()),
        out_specs=P("pcol", "prow"),
        check_vma=False,
    )
```

profile of v0, /device:TPU:1, one launch (start us, length us, event | category | flops | bytes accessed | tf_op | source)
XLA Modules:
  0.0 148.4 jit_solution(318537297239091147)
XLA Ops:
  6.5 0.0 copy-start
  6.5 0.0 all-gather.3.cloned.1.call-start
  6.5 1.0 slice.46
  7.6 0.7 collective-permute-start
  8.3 0.7 collective-permute-start.1
  8.9 1.3 collective-permute-start.2
  10.3 3.2 %fusion.20 = (f32[512,512]{1,0:T(8,128)}, f32[512,512]{1,0:T(8,128)}) fusion(f32[1024,512]{1,0:T(8,128)} %param.4), kind=kLoop, calls=%fused_computation.33 | loop fusion | bytes 4194304 | tf_op jit(solution)/shard_map/slice | solution.py:37
  13.4 0.0 collective-permute-done
  13.4 0.0 collective-permute-done.1
  13.4 2.6 %collective-permute-done.2 = f32[128,512]{1,0:T(8,128)S(1)} collective-permute-done((f32[128,512]{1,0:T(8,128)S(1)}, f32[128,512]{1,0:T(8,128)S(1)}, u32[]{:S(2)}, u32[]{:S(2)}) %collective-permute-start.2) | collective-permute-done | bytes 262176 | tf_op jit(solution)/shard_map/ppermute | solution.py:36
  16.0 0.0 copy-done
  16.0 0.1 select_select_fusion.4
  16.1 0.0 all-gather.3.cloned.1.call-update
  16.1 0.0 all-gather.5.cloned.1.call-start
  16.2 51.6 %all-gather.3.cloned.1.call-done = f32[512,2048]{1,0:T(8,128)} async-done(((f32[512,512]{1,0:T(8,128)}), f32[512,2048]{1,0:T(8,128)}) %all-gather.3.cloned.1.call-update) | async-done | bytes 4194320 | tf_op jit(solution)/shard_map/all_gather | solution.py:38
  67.7 0.0 all-gather.5.cloned.1.call-update
  67.7 2.4 %fusion.11 = f32[128,512]{1,0:T(8,128)S(1)} fusion(f32[128,512]{1,0:T(8,128)S(1)} %select_select_fusion.4, f32[2048,512]{1,0:T(8,128)} %param.5), kind=kOutput, calls=%fused_computation.17 | convolution fusion | flops 402653184 | bytes 1572864 | tf_op jit(solution)/shard_map/dot_general | solution.py:8
  70.1 2.4 %fusion.4 = f32[128,512]{1,0:T(8,128)S(1)} fusion(f32[128,512]{1,0:T(8,128)S(1)} %fusion.11, f32[512,2048]{1,0:T(8,128)} %all-gather.3.cloned.1.call-done), kind=kOutput, calls=%fused_computation.9 | convolution fusion | flops 402653184 | bytes 1572864 | tf_op jit(solution)/shard_map/dot_general | solution.py:8
  72.5 2.4 %fusion.9 = f32[128,512]{1,0:T(8,128)S(1)} fusion(f32[2048,512]{1,0:T(8,128)} %param.5, f32[128,512]{1,0:T(8,128)S(1)} %fusion.4, f32[128,1024]{1,0:T(8,128)S(1)} %copy-done), kind=kOutput, calls=%fused_computation.15 | convolution fusion | flops 402718720 | bytes 1835008 | tf_op jit(solution)/shard_map/dot_general | solution.py:8
  74.9 3.8 %collective-permute-start.3 = (f32[128,512]{1,0:T(8,128)S(1)}, f32[128,512]{1,0:T(8,128)S(1)}, u32[]{:S(2)}, u32[]{:S(2)}) collective-permute-start(f32[128,512]{1,0:T(8,128)S(1)} %fusion.9), channel_id=1, source_target_pairs={{4,8},{5,9},{6,10},{7,11}} | collective-permute-start | bytes 786440 | tf_op jit(solution)/shard_map/ppermute | solution.py:59
  78.7 1.3 collective-permute-start.4
  80.0 2.0 %collective-permute-done.3 = f32[128,512]{1,0:T(8,128)S(1)} collective-permute-done((f32[128,512]{1,0:T(8,128)S(1)}, f32[128,512]{1,0:T(8,128)S(1)}, u32[]{:S(2)}, u32[]{:S(2)}) %collective-permute-start.3) | collective-permute-done | bytes 262176 | tf_op jit(solution)/shard_map/ppermute | solution.py:59
  82.0 2.8 %collective-permute-done.4 = f32[128,512]{1,0:T(8,128)S(1)} collective-permute-done((f32[128,512]{1,0:T(8,128)S(1)}, f32[128,512]{1,0:T(8,128)S(1)}, u32[]{:S(2)}, u32[]{:S(2)}) %collective-permute-start.4) | collective-permute-done | bytes 262176 | tf_op jit(solution)/shard_map/ppermute | solution.py:59
  84.8 2.4 %convolution_add_fusion.1 = f32[128,512]{1,0:T(8,128)S(1)} fusion(f32[128,512]{1,0:T(8,128)S(1)} %fusion.4, f32[512,2048]{1,0:T(8,128)} %all-gather.3.cloned.1.call-done, f32[128,512]{1,0:T(8,128)S(1)} %collective-permute-done.3, f32[128,512]{1,0:T(8,128)S(1)} %collective-permute-done.4), kind=kOutput, calls=%fused_computation.6 | convolution fusion | flops 402784256 | bytes 2097152 | tf_op jit(solution)/shard_map/dot_general | solution.py:8
  87.3 2.4 %select_select_fusion.3 = (f32[128,512]{1,0:T(8,128)S(1)}, f32[128,512]{1,0:T(8,128)S(1)}) fusion(f32[128,512]{1,0:T(8,128)S(1)} %fusion.9, f32[128,512]{1,0:T(8,128)S(1)} %fusion.11, pred[]{:T(512)S(6)} %eq.71, pred[]{:T(512)S(6)} %eq.70, pred[]{:T(512)S(6)} %eq.69, f32[2048,512]{1,0:T(8,128)} %param.5, f32[128,512]{1,0:T(8,128)S(1)} %convolution_add_fusion.1, ...), kind=kOutput, calls=%fused_computation.24 | convolution fusion | flops 402915328 | bytes 2621443 | tf_op jit(solution)/shard_map/dot_general | solution.py:8
  89.7 0.7 collective-permute-start.5
  90.4 1.3 collective-permute-start.12
  91.7 1.3 collective-permute-start.13
  93.0 1.3 collective-permute-start.14
  94.4 0.0 collective-permute-done.5
  94.4 2.4 %fusion.1 = f32[128,512]{1,0:T(8,128)S(1)} fusion(f32[128,512]{1,0:T(8,128)S(1)} %convolution_add_fusion.1, f32[128,512]{1,0:T(8,128)S(1)} %collective-permute-done.5, f32[512,2048]{1,0:T(8,128)} %all-gather.3.cloned.1.call-done, f32[128,1024]{1,0:T(8,128)S(1)} %copy-done), kind=kOutput, calls=%fused_computation.5 | convolution fusion | flops 402784256 | bytes 2097152 | tf_op jit(solution)/shard_map/dot_general | solution.py:8
  96.8 2.4 %convolution_select_fusion = f32[128,512]{1,0:T(8,128)S(1)} fusion(f32[128,512]{1,0:T(8,128)S(1)} %get-tuple-element.17, f32[128,512]{1,0:T(8,128)S(1)} %fusion.1, f32[2048,512]{1,0:T(8,128)} %param.5, pred[]{:T(512)S(6)} %eq.68), kind=kOutput, calls=%fused_computation.3 | convolution fusion | flops 402718720 | bytes 1835009 | tf_op jit(solution)/shard_map/dot_general | solution.py:8
  99.2 0.7 collective-permute-start.6
  99.9 0.7 collective-permute-start.7
  100.5 0.0 collective-permute-done.12
  100.5 0.7 collective-permute-start.8
  101.2 0.0 collective-permute-done.13
  101.2 0.0 collective-permute-done.14
  101.3 0.1 select_select_fusion.1
  101.4 1.3 collective-permute-start.15
  102.7 1.3 collective-permute-start.16
  104.0 0.0 collective-permute-done.6
  104.0 1.3 collective-permute-start.17
  105.3 0.0 collective-permute-done.7
  105.3 0.0 collective-permute-done.8
  105.3 0.1 select_select_fusion.2
  105.4 0.7 collective-permute-start.10
  106.1 0.7 collective-permute-start.11
  106.8 0.0 collective-permute-done.15
  106.8 0.7 collective-permute-start.9
  107.5 1.0 collective-permute-done.16
  108.5 2.9 %collective-permute-done.17 = f32[128,512]{1,0:T(8,128)S(1)} collective-permute-done((f32[128,512]{1,0:T(8,128)S(1)}, f32[128,512]{1,0:T(8,128)S(1)}, u32[]{:S(2)}, u32[]{:S(2)}) %collective-permute-start.17) | collective-permute-done | bytes 262176 | tf_op jit(solution)/shard_map/ppermute | solution.py:70
  111.4 0.0 collective-permute-done.10
  111.4 0.0 collective-permute-done.11
  111.4 0.0 collective-permute-done.9
  111.4 0.2 select_select_fusion
  111.6 6.9 %collective-permute-start.18 = (f32[128,512]{1,0:T(8,128)S(1)}, f32[128,512]{1,0:T(8,128)S(1)}, u32[]{:S(2)}, u32[]{:S(2)}) collective-permute-start(f32[128,512]{1,0:T(8,128)S(1)} %select_select_fusion), channel_id=1, source_target_pairs={{0,8},{4,12},{8,0},{12,4},{16,24},{20,28},{24,16},{28,20},{32,40},... | collective-permute-start | bytes 786440 | tf_op jit(solution)/shard_map/ppermute | solution.py:77
  118.6 6.5 %collective-permute-done.18 = f32[128,512]{1,0:T(8,128)S(1)} collective-permute-done((f32[128,512]{1,0:T(8,128)S(1)}, f32[128,512]{1,0:T(8,128)S(1)}, u32[]{:S(2)}, u32[]{:S(2)}) %collective-permute-start.18) | collective-permute-done | bytes 262176 | tf_op jit(solution)/shard_map/ppermute | solution.py:77
  125.2 1.0 collective-permute-start.19
  126.2 1.5 %collective-permute-done.19 = f32[128,1024]{1,0:T(8,128)S(1)} collective-permute-done((f32[128,1024]{1,0:T(8,128)S(1)}, f32[128,1024]{1,0:T(8,128)S(1)}, u32[]{:S(2)}, u32[]{:S(2)}) %collective-permute-start.19) | collective-permute-done | bytes 524320 | tf_op jit(solution)/shard_map/ppermute | solution.py:81
  127.7 6.5 %fusion = f32[128,512]{1,0:T(8,128)S(1)} fusion(f32[128,512]{1,0:T(8,128)S(1)} %convolution_select_fusion, f32[512,2048]{1,0:T(8,128)} %all-gather.3.cloned.1.call-done, pred[]{:T(512)S(6)} %lt.61, f32[128,512]{1,0:T(8,128)S(1)} %get-tuple-element.16, f32[128,512]{1,0:T(8,128)S(1)} %get-tuple-element.14, f32[128,512]{1,0:T(8,128)S(1)} %get-tuple-element.15, ...), kind=kOutput, calls=%fused_computation.2 | convolution fusion | flops 1612578816 | bytes 6029314 | tf_op jit(solution)/shard_map/dot_general | solution.py:8
  134.2 0.0 all-gather.5.cloned.1.call-done
  134.3 6.5 %convolution_subtract_fusion = f32[128,512]{1,0:T(8,128)S(1)} fusion(f32[512,2048]{1,0:T(8,128)} %all-gather.5.cloned.1.call-done, f32[128,1024]{1,0:T(8,128)S(1)} %copy-done, f32[128,512]{1,0:T(8,128)S(1)} %get-tuple-element.16, f32[128,512]{1,0:T(8,128)S(1)} %get-tuple-element.14, f32[128,512]{1,0:T(8,128)S(1)} %get-tuple-element.15, ...), kind=kOutput, calls=%fused_computation | convolution fusion | flops 1612513280 | bytes 5767169 | tf_op jit(solution)/shard_map/dot_general | solution.py:8
  140.8 0.8 pad_maximum_fusion
  (3 shorter events, 0.1 us)
Async XLA Ops:
  6.5 9.5 %copy-start = (f32[128,1024]{1,0:T(8,128)S(1)}, f32[128,1024]{1,0:T(8,128)}, u32[]{:S(2)}) copy-start(f32[128,1024]{1,0:T(8,128)} %param.3) | copy-start | bytes 1572868
  6.5 61.2 %all-gather.3.cloned.1.call-start = ((), (), s32[]{:S(2)}) async-start(), calls=%async_computation | async-start | bytes 5242880 | tf_op jit(solution)/shard_map/all_gather | solution.py:38
  7.6 5.9 %collective-permute-start = (f32[128,512]{1,0:T(8,128)S(1)}, f32[128,512]{1,0:T(8,128)S(1)}, u32[]{:S(2)}, u32[]{:S(2)}) collective-permute-start(f32[128,512]{1,0:T(8,128)S(1)} %slice.46), channel_id=1, source_target_pairs={{0,12},{1,13},{2,14},{3,15}} | collective-permute-start | bytes 786440 | tf_op jit(solution)/shard_map/ppermute | solution.py:36
  8.3 5.2 %collective-permute-start.1 = (f32[128,512]{1,0:T(8,128)S(1)}, f32[128,512]{1,0:T(8,128)S(1)}, u32[]{:S(2)}, u32[]{:S(2)}) collective-permute-start(f32[128,512]{1,0:T(8,128)S(1)} %slice.46), channel_id=1, source_target_pairs={{0,8},{1,9},{2,10},{3,11}} | collective-permute-start | bytes 786440 | tf_op jit(solution)/shard_map/ppermute | solution.py:36
  8.9 7.0 %collective-permute-start.2 = (f32[128,512]{1,0:T(8,128)S(1)}, f32[128,512]{1,0:T(8,128)S(1)}, u32[]{:S(2)}, u32[]{:S(2)}) collective-permute-start(f32[128,512]{1,0:T(8,128)S(1)} %slice.46), channel_id=1, source_target_pairs={{0,4},{1,5},{2,6},{3,7}} | collective-permute-start | bytes 786440 | tf_op jit(solution)/shard_map/ppermute | solution.py:36
  16.1 118.1 %all-gather.5.cloned.1.call-start = ((), (), s32[]{:S(2)}) async-start(), calls=%async_computation.1 | async-start | bytes 5242880 | tf_op jit(solution)/shard_map/all_gather | solution.py:40
  74.9 7.1 %collective-permute-start.3 = (f32[128,512]{1,0:T(8,128)S(1)}, f32[128,512]{1,0:T(8,128)S(1)}, u32[]{:S(2)}, u32[]{:S(2)}) collective-permute-start(f32[128,512]{1,0:T(8,128)S(1)} %fusion.9), channel_id=1, source_target_pairs={{4,8},{5,9},{6,10},{7,11}} | collective-permute-start | bytes 786440 | tf_op jit(solution)/shard_map/ppermute | solution.py:59
  78.7 6.1 %collective-permute-start.4 = (f32[128,512]{1,0:T(8,128)S(1)}, f32[128,512]{1,0:T(8,128)S(1)}, u32[]{:S(2)}, u32[]{:S(2)}) collective-permute-start(f32[128,512]{1,0:T(8,128)S(1)} %fusion.9), channel_id=1, source_target_pairs={{4,12},{5,13},{6,14},{7,15}} | collective-permute-start | bytes 786440 | tf_op jit(solution)/shard_map/ppermute | solution.py:59
  89.7 4.7 %collective-permute-start.5 = (f32[128,512]{1,0:T(8,128)S(1)}, f32[128,512]{1,0:T(8,128)S(1)}, u32[]{:S(2)}, u32[]{:S(2)}) collective-permute-start(f32[128,512]{1,0:T(8,128)S(1)} %get-tuple-element.18), channel_id=1, source_target_pairs={{8,12},{9,13},{10,14},{11,15}} | collective-permute-start | bytes 786440 | tf_op jit(solution)/shard_map/ppermute | solution.py:59
  90.4 10.1 %collective-permute-start.12 = (f32[128,512]{1,0:T(8,128)S(1)}, f32[128,512]{1,0:T(8,128)S(1)}, u32[]{:S(2)}, u32[]{:S(2)}) collective-permute-start(f32[128,512]{1,0:T(8,128)S(1)} %get-tuple-element.17), channel_id=1, source_target_pairs={{0,192},{4,196},{8,200},{1,193},{5,197},{9,201},{2,194},{6,198},{1... | collective-permute-start | bytes 786440 | tf_op jit(solution)/shard_map/ppermute | solution.py:70
  91.7 9.5 %collective-permute-start.13 = (f32[128,512]{1,0:T(8,128)S(1)}, f32[128,512]{1,0:T(8,128)S(1)}, u32[]{:S(2)}, u32[]{:S(2)}) collective-permute-start(f32[128,512]{1,0:T(8,128)S(1)} %get-tuple-element.17), channel_id=1, source_target_pairs={{0,64},{4,68},{8,72},{1,65},{5,69},{9,73},{2,66},{6,70},{10,74},{3... | collective-permute-start | bytes 786440 | tf_op jit(solution)/shard_map/ppermute | solution.py:70
  93.0 8.2 %collective-permute-start.14 = (f32[128,512]{1,0:T(8,128)S(1)}, f32[128,512]{1,0:T(8,128)S(1)}, u32[]{:S(2)}, u32[]{:S(2)}) collective-permute-start(f32[128,512]{1,0:T(8,128)S(1)} %get-tuple-element.17), channel_id=1, source_target_pairs={{0,128},{4,132},{8,136},{1,129},{5,133},{9,137},{2,130},{6,134},{1... | collective-permute-start | bytes 786440 | tf_op jit(solution)/shard_map/ppermute | solution.py:70
  99.2 4.8 %collective-permute-start.6 = (f32[128,512]{1,0:T(8,128)S(1)}, f32[128,512]{1,0:T(8,128)S(1)}, u32[]{:S(2)}, u32[]{:S(2)}) collective-permute-start(f32[128,512]{1,0:T(8,128)S(1)} %convolution_select_fusion), channel_id=1, source_target_pairs={{12,204},{13,205},{14,206},{15,207}} | collective-permute-start | bytes 786440 | tf_op jit(solution)/shard_map/ppermute | solution.py:70
  99.9 5.5 %collective-permute-start.7 = (f32[128,512]{1,0:T(8,128)S(1)}, f32[128,512]{1,0:T(8,128)S(1)}, u32[]{:S(2)}, u32[]{:S(2)}) collective-permute-start(f32[128,512]{1,0:T(8,128)S(1)} %convolution_select_fusion), channel_id=1, source_target_pairs={{12,76},{13,77},{14,78},{15,79}} | collective-permute-start | bytes 786440 | tf_op jit(solution)/shard_map/ppermute | solution.py:70
  100.5 4.8 %collective-permute-start.8 = (f32[128,512]{1,0:T(8,128)S(1)}, f32[128,512]{1,0:T(8,128)S(1)}, u32[]{:S(2)}, u32[]{:S(2)}) collective-permute-start(f32[128,512]{1,0:T(8,128)S(1)} %convolution_select_fusion), channel_id=1, source_target_pairs={{12,140},{13,141},{14,142},{15,143}} | collective-permute-start | bytes 786440 | tf_op jit(solution)/shard_map/ppermute | solution.py:70
  101.4 5.4 %collective-permute-start.15 = (f32[128,512]{1,0:T(8,128)S(1)}, f32[128,512]{1,0:T(8,128)S(1)}, u32[]{:S(2)}, u32[]{:S(2)}) collective-permute-start(f32[128,512]{1,0:T(8,128)S(1)} %select_select_fusion.1), channel_id=1, source_target_pairs={{0,48},{4,52},{8,56},{64,112},{68,116},{72,120},{128,176},{132,180... | collective-permute-start | bytes 786440 | tf_op jit(solution)/shard_map/ppermute | solution.py:70
  102.7 5.9 %collective-permute-start.16 = (f32[128,512]{1,0:T(8,128)S(1)}, f32[128,512]{1,0:T(8,128)S(1)}, u32[]{:S(2)}, u32[]{:S(2)}) collective-permute-start(f32[128,512]{1,0:T(8,128)S(1)} %select_select_fusion.1), channel_id=1, source_target_pairs={{0,16},{4,20},{8,24},{64,80},{68,84},{72,88},{128,144},{132,148},{... | collective-permute-start | bytes 786440 | tf_op jit(solution)/shard_map/ppermute | solution.py:70
  104.0 7.4 %collective-permute-start.17 = (f32[128,512]{1,0:T(8,128)S(1)}, f32[128,512]{1,0:T(8,128)S(1)}, u32[]{:S(2)}, u32[]{:S(2)}) collective-permute-start(f32[128,512]{1,0:T(8,128)S(1)} %select_select_fusion.1), channel_id=1, source_target_pairs={{0,32},{4,36},{8,40},{64,96},{68,100},{72,104},{128,160},{132,164}... | collective-permute-start | bytes 786440 | tf_op jit(solution)/shard_map/ppermute | solution.py:70
  105.4 5.9 %collective-permute-start.10 = (f32[128,512]{1,0:T(8,128)S(1)}, f32[128,512]{1,0:T(8,128)S(1)}, u32[]{:S(2)}, u32[]{:S(2)}) collective-permute-start(f32[128,512]{1,0:T(8,128)S(1)} %select_select_fusion.2), channel_id=1, source_target_pairs={{12,28},{76,92},{140,156},{204,220},{13,29},{77,93},{141,157},{205... | collective-permute-start | bytes 786440 | tf_op jit(solution)/shard_map/ppermute | solution.py:70
  106.1 5.3 %collective-permute-start.11 = (f32[128,512]{1,0:T(8,128)S(1)}, f32[128,512]{1,0:T(8,128)S(1)}, u32[]{:S(2)}, u32[]{:S(2)}) collective-permute-start(f32[128,512]{1,0:T(8,128)S(1)} %select_select_fusion.2), channel_id=1, source_target_pairs={{12,44},{76,108},{140,172},{204,236},{13,45},{77,109},{141,173},{2... | collective-permute-start | bytes 786440 | tf_op jit(solution)/shard_map/ppermute | solution.py:70
  106.8 4.6 %collective-permute-start.9 = (f32[128,512]{1,0:T(8,128)S(1)}, f32[128,512]{1,0:T(8,128)S(1)}, u32[]{:S(2)}, u32[]{:S(2)}) collective-permute-start(f32[128,512]{1,0:T(8,128)S(1)} %select_select_fusion.2), channel_id=1, source_target_pairs={{12,60},{76,124},{140,188},{204,252},{13,61},{77,125},{141,189},{2... | collective-permute-start | bytes 786440 | tf_op jit(solution)/shard_map/ppermute | solution.py:70
  111.6 13.5 %collective-permute-start.18 = (f32[128,512]{1,0:T(8,128)S(1)}, f32[128,512]{1,0:T(8,128)S(1)}, u32[]{:S(2)}, u32[]{:S(2)}) collective-permute-start(f32[128,512]{1,0:T(8,128)S(1)} %select_select_fusion), channel_id=1, source_target_pairs={{0,8},{4,12},{8,0},{12,4},{16,24},{20,28},{24,16},{28,20},{32,40},... | collective-permute-start | bytes 786440 | tf_op jit(solution)/shard_map/ppermute | solution.py:77
  125.2 2.5 %collective-permute-start.19 = (f32[128,1024]{1,0:T(8,128)S(1)}, f32[128,1024]{1,0:T(8,128)S(1)}, u32[]{:S(2)}, u32[]{:S(2)}) collective-permute-start(f32[128,1024]{1,0:T(8,128)S(1)} %maximum_select_fusion.1), channel_id=1, source_target_pairs={{0,4},{4,0},{8,12},{12,8},{16,20},{20,16},{24,28},{28,24},{32,36},... | collective-permute-start | bytes 1572872 | tf_op jit(solution)/shard_map/ppermute | solution.py:81
Sparse Core Ops, SparseCore 0:
  16.2 51.4 all-gather.2
  69.5 51.1 all-gather.4
where the time goes:
time: 149 us; the launch traced here: 148 us
  waiting for transfers between devices  70.9 us (48%)
  matrix products  29.8 us (20%)
  starting transfers between devices  28.3 us (19%)
  between operations  13.8 us (9%)
  local copies, waits for them, and re-layouts  4.28 us (3%)
    all_gather x1, waiting for transfers between devices, per_device(): lower_first = lax.all_gather(first_rows, 'pcol', axis=1, tiled=True)  51.6 us
    dot_general x9, matrix products, contract(): lax.dot_general(left, right, (((1,), (1,)), ((), ())), precision=lax.Prec...  29.8 us
    ppermute x12, starting transfers between devices, per_device(): arrived = lax.ppermute(piece, 'prow', pairs)  11.9 us
    ppermute x1, starting transfers between devices, per_device(): other = lax.ppermute(piece, 'prow', [(p, p ^ 2) for p in range(n_row)])  6.93 us
    ppermute x1, waiting for transfers between devices, per_device(): other = lax.ppermute(piece, 'prow', [(p, p ^ 2) for p in range(n_row)])  6.55 us
    ppermute x3, starting transfers between devices, per_device(): arrived = arrived + lax.ppermute(solved, AXES, pairs)  5.78 us
    ppermute x3, waiting for transfers between devices, per_device(): arrived = arrived + lax.ppermute(solved, AXES, pairs)  4.78 us
    ppermute x12, waiting for transfers between devices, per_device(): arrived = lax.ppermute(piece, 'prow', pairs)  3.86 us
  transfers between devices with their start and end apart: 22, of which 8 were waited for; matrix products, arithmetic and copies ran while one was open for 18% of the time, Pallas kernels for 0%

commit v1 on v0

--- a/solution.py
+++ b/solution.py
@@ -35,7 +35,9 @@
         pairs = [(at(0, c), at(i, c)) for c in range(n_col)]
         first_rhs = jnp.where(row_at == i, lax.ppermute(top_rhs, AXES, pairs), first_rhs)
     first_rhs, first_rows = lax.optimization_barrier((first_rhs, factor[:block]))
-    lower_first = lax.all_gather(first_rows, "pcol", axis=1, tiled=True)
+    lower_first = jnp.concatenate(
+        lax.all_to_all(jnp.stack([first_rows] * lax.axis_size("pcol")), "pcol", 0, 0), axis=1
+    )
     second_rows, _ = lax.optimization_barrier((factor[block:], lower_first))
     lower_second = lax.all_gather(second_rows, "pcol", axis=1, tiled=True)
     acc = jnp.zeros((rhs_width, block), jnp.float32)

time: 149 us -> 148 us (level)
  waiting for transfers between devices: 70.9 us -> 17.6 us
  blocking collectives: 0 us -> 49.6 us
  starting transfers between devices: 28.3 us -> 33.5 us
  matrix products: 29.8 us -> 26.6 us
    all_gather x1 -> x0, waiting for transfers between devices: 51.6 us -> none  [per_device(): lower_first = lax.all_gather(first_rows, 'pcol', axis=1, tiled=True)]
    all_to_all x0 -> x1, blocking collectives: none -> 49.6 us  [per_device(): lax.all_to_all(jnp.stack([first_rows] * lax.axis_size('pcol')), 'pcol', 0...]
    ppermute x3, starting transfers between devices: 5.78 us -> 9.8 us  [per_device(): arrived = arrived + lax.ppermute(solved, AXES, pairs)]
    dot_general x9, matrix products: 29.8 us -> 26.6 us  [contract(): lax.dot_general(left, right, (((1,), (1,)), ((), ())), precision=lax.Prec...]
    ppermute x1, starting transfers between devices: 6.93 us -> 8.92 us  [per_device(): other = lax.ppermute(piece, 'prow', [(p, p ^ 2) for p in range(n_row)])]
  transfers between devices with their start and end apart: 22 -> 21, of which waited for: 8 -> 6; matrix products, arithmetic and copies ran while one was open for 18% -> 16% of each run, Pallas kernels for 0% -> 0%
where the time goes in v1:
time: 148 us; the launch traced here: 147 us
  blocking collectives  49.6 us (34%)
  starting transfers between devices  33.5 us (23%)
  matrix products  26.6 us (18%)
  waiting for transfers between devices  17.6 us (12%)
  between operations  13.9 us (9%)
  local copies, waits for them, and re-layouts  4.74 us (3%)
    all_to_all x1, blocking collectives, per_device(): lax.all_to_all(jnp.stack([first_rows] * lax.axis_size('pcol')), 'pcol', 0...  49.6 us
    dot_general x9, matrix products, contract(): lax.dot_general(left, right, (((1,), (1,)), ((), ())), precision=lax.Prec...  26.6 us
    ppermute x12, starting transfers between devices, per_device(): arrived = lax.ppermute(piece, 'prow', pairs)  11.9 us
    ppermute x3, starting transfers between devices, per_device(): arrived = arrived + lax.ppermute(solved, AXES, pairs)  9.8 us
    ppermute x1, starting transfers between devices, per_device(): other = lax.ppermute(piece, 'prow', [(p, p ^ 2) for p in range(n_row)])  8.92 us
    ppermute x1, waiting for transfers between devices, per_device(): other = lax.ppermute(piece, 'prow', [(p, p ^ 2) for p in range(n_row)])  5.39 us
    ppermute x3, waiting for transfers between devices, per_device(): arrived = arrived + lax.ppermute(solved, AXES, pairs)  4.78 us
  transfers between devices with their start and end apart: 21, of which 6 were waited for; matrix products, arithmetic and copies ran while one was open for 16% of the time, Pallas kernels for 0%

profile of v1, /device:TPU:1, one launch (start us, length us, event | category | flops | bytes accessed | tf_op | source)
XLA Modules:
  0.0 147.3 jit_solution(13922081473330476234)
XLA Ops:
  6.5 0.0 copy-start
  6.5 0.0 all-gather.2.cloned.1.call-start
  6.5 1.0 slice.46
  7.6 0.7 collective-permute-start
  8.3 0.7 collective-permute-start.1
  8.9 1.3 collective-permute-start.2
  10.3 2.8 %fusion.20 = (f32[512,512]{1,0:T(8,128)S(1)}, f32[512,512]{1,0:T(8,128)}) fusion(f32[1024,512]{1,0:T(8,128)} %param.4), kind=kLoop, calls=%fused_computation.33 | loop fusion | bytes 4194304 | tf_op jit(solution)/shard_map/slice | solution.py:37
  13.0 0.0 collective-permute-done
  13.0 0.0 collective-permute-done.1
  13.1 2.9 %collective-permute-done.2 = f32[128,512]{1,0:T(8,128)S(1)} collective-permute-done((f32[128,512]{1,0:T(8,128)S(1)}, f32[128,512]{1,0:T(8,128)S(1)}, u32[]{:S(2)}, u32[]{:S(2)}) %collective-permute-start.2) | collective-permute-done | bytes 262176 | tf_op jit(solution)/shard_map/ppermute | solution.py:36
  16.0 0.0 copy-done
  16.0 0.1 select_select_fusion.4
  16.1 0.3 copy.4
  16.4 0.5 stack.2
  16.9 49.6 %all_to_all.5 = f32[4,512,512]{1,2,0:T(8,128)} all-to-all(f32[4,512,512]{1,2,0:T(8,128)S(1)} %stack.2), channel_id=1, replica_groups=mesh['prow'=64,'pcol'=4] {'pcol'}, dimensions={0} | all-to-all | bytes 8388608 | tf_op jit(solution)/shard_map/all_to_all | solution.py:39
  66.5 0.0 all-gather.2.cloned.1.call-update
  66.6 2.4 %fusion.11 = f32[128,512]{1,0:T(8,128)S(1)} fusion(f32[128,512]{1,0:T(8,128)S(1)} %select_select_fusion.4, f32[2048,512]{1,0:T(8,128)} %param.5), kind=kOutput, calls=%fused_computation.17 | convolution fusion | flops 402653184 | bytes 1572864 | tf_op jit(solution)/shard_map/dot_general | solution.py:8
  69.0 1.9 %fusion.4 = f32[128,512]{1,0:T(8,128)S(1)} fusion(f32[128,512]{1,0:T(8,128)S(1)} %fusion.11, f32[512,2048]{0,1:T(8,128)} %bitcast.9), kind=kOutput, calls=%fused_computation.9 | convolution fusion | flops 402653184 | bytes 1572864 | tf_op jit(solution)/shard_map/dot_general | solution.py:8
  70.9 2.4 %fusion.9 = f32[128,512]{1,0:T(8,128)S(1)} fusion(f32[2048,512]{1,0:T(8,128)} %param.5, f32[128,512]{1,0:T(8,128)S(1)} %fusion.4, f32[128,1024]{1,0:T(8,128)S(1)} %copy-done), kind=kOutput, calls=%fused_computation.15 | convolution fusion | flops 402718720 | bytes 1835008 | tf_op jit(solution)/shard_map/dot_general | solution.py:8
  73.3 7.8 %collective-permute-start.3 = (f32[128,512]{1,0:T(8,128)S(1)}, f32[128,512]{1,0:T(8,128)S(1)}, u32[]{:S(2)}, u32[]{:S(2)}) collective-permute-start(f32[128,512]{1,0:T(8,128)S(1)} %fusion.9), channel_id=1, source_target_pairs={{4,8},{5,9},{6,10},{7,11}} | collective-permute-start | bytes 786440 | tf_op jit(solution)/shard_map/ppermute | solution.py:61
  81.1 1.3 collective-permute-start.4
  82.4 2.0 %collective-permute-done.3 = f32[128,512]{1,0:T(8,128)S(1)} collective-permute-done((f32[128,512]{1,0:T(8,128)S(1)}, f32[128,512]{1,0:T(8,128)S(1)}, u32[]{:S(2)}, u32[]{:S(2)}) %collective-permute-start.3) | collective-permute-done | bytes 262176 | tf_op jit(solution)/shard_map/ppermute | solution.py:61
  84.4 2.8 %collective-permute-done.4 = f32[128,512]{1,0:T(8,128)S(1)} collective-permute-done((f32[128,512]{1,0:T(8,128)S(1)}, f32[128,512]{1,0:T(8,128)S(1)}, u32[]{:S(2)}, u32[]{:S(2)}) %collective-permute-start.4) | collective-permute-done | bytes 262176 | tf_op jit(solution)/shard_map/ppermute | solution.py:61
  87.2 1.9 %convolution_add_fusion.1 = f32[128,512]{1,0:T(8,128)S(1)} fusion(f32[128,512]{1,0:T(8,128)S(1)} %fusion.4, f32[512,2048]{0,1:T(8,128)} %bitcast.10, f32[128,512]{1,0:T(8,128)S(1)} %collective-permute-done.3, f32[128,512]{1,0:T(8,128)S(1)} %collective-permute-done.4), kind=kOutput, calls=%fused_computation.6 | convolution fusion | flops 402784256 | bytes 2097152 | tf_op jit(solution)/shard_map/dot_general | solution.py:8
  89.2 2.4 %select_select_fusion.3 = (f32[128,512]{1,0:T(8,128)S(1)}, f32[128,512]{1,0:T(8,128)S(1)}) fusion(f32[128,512]{1,0:T(8,128)S(1)} %fusion.9, f32[128,512]{1,0:T(8,128)S(1)} %fusion.11, pred[]{:T(512)S(6)} %eq.71, pred[]{:T(512)S(6)} %eq.70, pred[]{:T(512)S(6)} %eq.69, f32[2048,512]{1,0:T(8,128)} %param.5, f32[128,512]{1,0:T(8,128)S(1)} %convolution_add_fusion.1, ...), kind=kOutput, calls=%fused_computation.24 | convolution fusion | flops 402915328 | bytes 2621443 | tf_op jit(solution)/shard_map/dot_general | solution.py:8
  91.6 0.7 collective-permute-start.5
  92.3 1.3 collective-permute-start.12
  93.6 1.3 collective-permute-start.13
  95.0 1.3 collective-permute-start.14
  96.3 0.0 collective-permute-done.5
  96.3 1.9 %fusion.1 = f32[128,512]{1,0:T(8,128)S(1)} fusion(f32[128,512]{1,0:T(8,128)S(1)} %convolution_add_fusion.1, f32[128,512]{1,0:T(8,128)S(1)} %collective-permute-done.5, f32[512,2048]{0,1:T(8,128)} %bitcast.11, f32[128,1024]{1,0:T(8,128)S(1)} %copy-done), kind=kOutput, calls=%fused_computation.5 | convolution fusion | flops 402784256 | bytes 2097152 | tf_op jit(solution)/shard_map/dot_general | solution.py:8
  98.2 2.4 %convolution_select_fusion = f32[128,512]{1,0:T(8,128)S(1)} fusion(f32[128,512]{1,0:T(8,128)S(1)} %get-tuple-element.17, f32[128,512]{1,0:T(8,128)S(1)} %fusion.1, f32[2048,512]{1,0:T(8,128)} %param.5, pred[]{:T(512)S(6)} %eq.68), kind=kOutput, calls=%fused_computation.3 | convolution fusion | flops 402718720 | bytes 1835009 | tf_op jit(solution)/shard_map/dot_general | solution.py:8
  100.6 0.7 collective-permute-start.6
  101.3 0.7 collective-permute-start.7
  102.0 0.0 collective-permute-done.12
  102.0 0.7 collective-permute-start.8
  102.7 0.0 collective-permute-done.13
  102.7 0.0 collective-permute-done.14
  102.7 0.1 select_select_fusion.1
  102.8 1.3 collective-permute-start.15
  104.1 1.3 collective-permute-start.16
  105.4 0.0 collective-permute-done.6
  105.5 1.3 collective-permute-start.17
  106.8 0.0 collective-permute-done.7
  106.8 0.0 collective-permute-done.8
  106.8 0.1 select_select_fusion.2
  106.9 0.7 collective-permute-start.10
  107.6 0.7 collective-permute-start.11
  108.3 0.0 collective-permute-done.15
  108.3 0.7 collective-permute-start.9
  109.0 0.0 collective-permute-done.16
  109.0 2.6 %collective-permute-done.17 = f32[128,512]{1,0:T(8,128)S(1)} collective-permute-done((f32[128,512]{1,0:T(8,128)S(1)}, f32[128,512]{1,0:T(8,128)S(1)}, u32[]{:S(2)}, u32[]{:S(2)}) %collective-permute-start.17) | collective-permute-done | bytes 262176 | tf_op jit(solution)/shard_map/ppermute | solution.py:72
  111.6 0.0 collective-permute-done.10
  111.6 0.0 collective-permute-done.11
  111.6 0.0 collective-permute-done.9
  111.6 0.2 select_select_fusion
  111.8 8.9 %collective-permute-start.18 = (f32[128,512]{1,0:T(8,128)S(1)}, f32[128,512]{1,0:T(8,128)S(1)}, u32[]{:S(2)}, u32[]{:S(2)}) collective-permute-start(f32[128,512]{1,0:T(8,128)S(1)} %select_select_fusion), channel_id=1, source_target_pairs={{0,8},{4,12},{8,0},{12,4},{16,24},{20,28},{24,16},{28,20},{32,40},... | collective-permute-start | bytes 786440 | tf_op jit(solution)/shard_map/ppermute | solution.py:79
  120.8 5.4 %collective-permute-done.18 = f32[128,512]{1,0:T(8,128)S(1)} collective-permute-done((f32[128,512]{1,0:T(8,128)S(1)}, f32[128,512]{1,0:T(8,128)S(1)}, u32[]{:S(2)}, u32[]{:S(2)}) %collective-permute-start.18) | collective-permute-done | bytes 262176 | tf_op jit(solution)/shard_map/ppermute | solution.py:79
  126.2 0.3 collective-permute-start.19
  126.5 1.8 %collective-permute-done.19 = f32[128,1024]{1,0:T(8,128)S(1)} collective-permute-done((f32[128,1024]{1,0:T(8,128)S(1)}, f32[128,1024]{1,0:T(8,128)S(1)}, u32[]{:S(2)}, u32[]{:S(2)}) %collective-permute-start.19) | collective-permute-done | bytes 524320 | tf_op jit(solution)/shard_map/ppermute | solution.py:83
  128.4 4.6 %fusion = f32[128,512]{1,0:T(8,128)S(1)} fusion(f32[128,512]{1,0:T(8,128)S(1)} %convolution_select_fusion, f32[512,2048]{0,1:T(8,128)} %bitcast.12, pred[]{:T(512)S(6)} %lt.61, f32[128,512]{1,0:T(8,128)S(1)} %get-tuple-element.16, f32[128,512]{1,0:T(8,128)S(1)} %get-tuple-element.14, f32[128,512]{1,0:T(8,128)S(1)} %get-tuple-element.15, ...), kind=kOutput, calls=%fused_computation.2 | convolution fusion | flops 1612578816 | bytes 6029314 | tf_op jit(solution)/shard_map/dot_general | solution.py:8
  133.1 0.0 all-gather.2.cloned.1.call-done
  133.1 6.5 %convolution_subtract_fusion = f32[128,512]{1,0:T(8,128)S(1)} fusion(f32[512,2048]{1,0:T(8,128)} %all-gather.2.cloned.1.call-done, f32[128,1024]{1,0:T(8,128)S(1)} %copy-done, f32[128,512]{1,0:T(8,128)S(1)} %get-tuple-element.16, f32[128,512]{1,0:T(8,128)S(1)} %get-tuple-element.14, f32[128,512]{1,0:T(8,128)S(1)} %get-tuple-element.15, ...), kind=kOutput, calls=%fused_computation | convolution fusion | flops 1612513280 | bytes 5767169 | tf_op jit(solution)/shard_map/dot_general | solution.py:8
  139.6 0.8 pad_maximum_fusion
  (3 shorter events, 0.1 us)
Async XLA Ops:
  6.5 9.5 %copy-start = (f32[128,1024]{1,0:T(8,128)S(1)}, f32[128,1024]{1,0:T(8,128)}, u32[]{:S(2)}) copy-start(f32[128,1024]{1,0:T(8,128)} %param.3) | copy-start | bytes 1572868
  6.5 126.6 %all-gather.2.cloned.1.call-start = ((), (), s32[]{:S(2)}) async-start(), calls=%async_computation.1 | async-start | bytes 5242880 | tf_op jit(solution)/shard_map/all_gather | solution.py:42
  7.6 5.5 %collective-permute-start = (f32[128,512]{1,0:T(8,128)S(1)}, f32[128,512]{1,0:T(8,128)S(1)}, u32[]{:S(2)}, u32[]{:S(2)}) collective-permute-start(f32[128,512]{1,0:T(8,128)S(1)} %slice.46), channel_id=1, source_target_pairs={{0,12},{1,13},{2,14},{3,15}} | collective-permute-start | bytes 786440 | tf_op jit(solution)/shard_map/ppermute | solution.py:36
  8.3 4.8 %collective-permute-start.1 = (f32[128,512]{1,0:T(8,128)S(1)}, f32[128,512]{1,0:T(8,128)S(1)}, u32[]{:S(2)}, u32[]{:S(2)}) collective-permute-start(f32[128,512]{1,0:T(8,128)S(1)} %slice.46), channel_id=1, source_target_pairs={{0,8},{1,9},{2,10},{3,11}} | collective-permute-start | bytes 786440 | tf_op jit(solution)/shard_map/ppermute | solution.py:36
  8.9 7.0 %collective-permute-start.2 = (f32[128,512]{1,0:T(8,128)S(1)}, f32[128,512]{1,0:T(8,128)S(1)}, u32[]{:S(2)}, u32[]{:S(2)}) collective-permute-start(f32[128,512]{1,0:T(8,128)S(1)} %slice.46), channel_id=1, source_target_pairs={{0,4},{1,5},{2,6},{3,7}} | collective-permute-start | bytes 786440 | tf_op jit(solution)/shard_map/ppermute | solution.py:36
  73.3 11.1 %collective-permute-start.3 = (f32[128,512]{1,0:T(8,128)S(1)}, f32[128,512]{1,0:T(8,128)S(1)}, u32[]{:S(2)}, u32[]{:S(2)}) collective-permute-start(f32[128,512]{1,0:T(8,128)S(1)} %fusion.9), channel_id=1, source_target_pairs={{4,8},{5,9},{6,10},{7,11}} | collective-permute-start | bytes 786440 | tf_op jit(solution)/shard_map/ppermute | solution.py:61
  81.1 6.1 %collective-permute-start.4 = (f32[128,512]{1,0:T(8,128)S(1)}, f32[128,512]{1,0:T(8,128)S(1)}, u32[]{:S(2)}, u32[]{:S(2)}) collective-permute-start(f32[128,512]{1,0:T(8,128)S(1)} %fusion.9), channel_id=1, source_target_pairs={{4,12},{5,13},{6,14},{7,15}} | collective-permute-start | bytes 786440 | tf_op jit(solution)/shard_map/ppermute | solution.py:61
  91.6 4.7 %collective-permute-start.5 = (f32[128,512]{1,0:T(8,128)S(1)}, f32[128,512]{1,0:T(8,128)S(1)}, u32[]{:S(2)}, u32[]{:S(2)}) collective-permute-start(f32[128,512]{1,0:T(8,128)S(1)} %get-tuple-element.18), channel_id=1, source_target_pairs={{8,12},{9,13},{10,14},{11,15}} | collective-permute-start | bytes 786440 | tf_op jit(solution)/shard_map/ppermute | solution.py:61
  92.3 9.7 %collective-permute-start.12 = (f32[128,512]{1,0:T(8,128)S(1)}, f32[128,512]{1,0:T(8,128)S(1)}, u32[]{:S(2)}, u32[]{:S(2)}) collective-permute-start(f32[128,512]{1,0:T(8,128)S(1)} %get-tuple-element.17), channel_id=1, source_target_pairs={{0,192},{4,196},{8,200},{1,193},{5,197},{9,201},{2,194},{6,198},{1... | collective-permute-start | bytes 786440 | tf_op jit(solution)/shard_map/ppermute | solution.py:72
  93.6 9.1 %collective-permute-start.13 = (f32[128,512]{1,0:T(8,128)S(1)}, f32[128,512]{1,0:T(8,128)S(1)}, u32[]{:S(2)}, u32[]{:S(2)}) collective-permute-start(f32[128,512]{1,0:T(8,128)S(1)} %get-tuple-element.17), channel_id=1, source_target_pairs={{0,64},{4,68},{8,72},{1,65},{5,69},{9,73},{2,66},{6,70},{10,74},{3... | collective-permute-start | bytes 786440 | tf_op jit(solution)/shard_map/ppermute | solution.py:72
  95.0 7.8 %collective-permute-start.14 = (f32[128,512]{1,0:T(8,128)S(1)}, f32[128,512]{1,0:T(8,128)S(1)}, u32[]{:S(2)}, u32[]{:S(2)}) collective-permute-start(f32[128,512]{1,0:T(8,128)S(1)} %get-tuple-element.17), channel_id=1, source_target_pairs={{0,128},{4,132},{8,136},{1,129},{5,133},{9,137},{2,130},{6,134},{1... | collective-permute-start | bytes 786440 | tf_op jit(solution)/shard_map/ppermute | solution.py:72
  100.6 4.8 %collective-permute-start.6 = (f32[128,512]{1,0:T(8,128)S(1)}, f32[128,512]{1,0:T(8,128)S(1)}, u32[]{:S(2)}, u32[]{:S(2)}) collective-permute-start(f32[128,512]{1,0:T(8,128)S(1)} %convolution_select_fusion), channel_id=1, source_target_pairs={{12,204},{13,205},{14,206},{15,207}} | collective-permute-start | bytes 786440 | tf_op jit(solution)/shard_map/ppermute | solution.py:72
  101.3 5.5 %collective-permute-start.7 = (f32[128,512]{1,0:T(8,128)S(1)}, f32[128,512]{1,0:T(8,128)S(1)}, u32[]{:S(2)}, u32[]{:S(2)}) collective-permute-start(f32[128,512]{1,0:T(8,128)S(1)} %convolution_select_fusion), channel_id=1, source_target_pairs={{12,76},{13,77},{14,78},{15,79}} | collective-permute-start | bytes 786440 | tf_op jit(solution)/shard_map/ppermute | solution.py:72
  102.0 4.8 %collective-permute-start.8 = (f32[128,512]{1,0:T(8,128)S(1)}, f32[128,512]{1,0:T(8,128)S(1)}, u32[]{:S(2)}, u32[]{:S(2)}) collective-permute-start(f32[128,512]{1,0:T(8,128)S(1)} %convolution_select_fusion), channel_id=1, source_target_pairs={{12,140},{13,141},{14,142},{15,143}} | collective-permute-start | bytes 786440 | tf_op jit(solution)/shard_map/ppermute | solution.py:72
  102.8 5.4 %collective-permute-start.15 = (f32[128,512]{1,0:T(8,128)S(1)}, f32[128,512]{1,0:T(8,128)S(1)}, u32[]{:S(2)}, u32[]{:S(2)}) collective-permute-start(f32[128,512]{1,0:T(8,128)S(1)} %select_select_fusion.1), channel_id=1, source_target_pairs={{0,48},{4,52},{8,56},{64,112},{68,116},{72,120},{128,176},{132,180... | collective-permute-start | bytes 786440 | tf_op jit(solution)/shard_map/ppermute | solution.py:72
  104.1 4.9 %collective-permute-start.16 = (f32[128,512]{1,0:T(8,128)S(1)}, f32[128,512]{1,0:T(8,128)S(1)}, u32[]{:S(2)}, u32[]{:S(2)}) collective-permute-start(f32[128,512]{1,0:T(8,128)S(1)} %select_select_fusion.1), channel_id=1, source_target_pairs={{0,16},{4,20},{8,24},{64,80},{68,84},{72,88},{128,144},{132,148},{... | collective-permute-start | bytes 786440 | tf_op jit(solution)/shard_map/ppermute | solution.py:72
  105.5 6.1 %collective-permute-start.17 = (f32[128,512]{1,0:T(8,128)S(1)}, f32[128,512]{1,0:T(8,128)S(1)}, u32[]{:S(2)}, u32[]{:S(2)}) collective-permute-start(f32[128,512]{1,0:T(8,128)S(1)} %select_select_fusion.1), channel_id=1, source_target_pairs={{0,32},{4,36},{8,40},{64,96},{68,100},{72,104},{128,160},{132,164}... | collective-permute-start | bytes 786440 | tf_op jit(solution)/shard_map/ppermute | solution.py:72
  106.9 4.7 %collective-permute-start.10 = (f32[128,512]{1,0:T(8,128)S(1)}, f32[128,512]{1,0:T(8,128)S(1)}, u32[]{:S(2)}, u32[]{:S(2)}) collective-permute-start(f32[128,512]{1,0:T(8,128)S(1)} %select_select_fusion.2), channel_id=1, source_target_pairs={{12,28},{76,92},{140,156},{204,220},{13,29},{77,93},{141,157},{205... | collective-permute-start | bytes 786440 | tf_op jit(solution)/shard_map/ppermute | solution.py:72
  107.6 4.0 %collective-permute-start.11 = (f32[128,512]{1,0:T(8,128)S(1)}, f32[128,512]{1,0:T(8,128)S(1)}, u32[]{:S(2)}, u32[]{:S(2)}) collective-permute-start(f32[128,512]{1,0:T(8,128)S(1)} %select_select_fusion.2), channel_id=1, source_target_pairs={{12,44},{76,108},{140,172},{204,236},{13,45},{77,109},{141,173},{2... | collective-permute-start | bytes 786440 | tf_op jit(solution)/shard_map/ppermute | solution.py:72
  108.3 3.3 %collective-permute-start.9 = (f32[128,512]{1,0:T(8,128)S(1)}, f32[128,512]{1,0:T(8,128)S(1)}, u32[]{:S(2)}, u32[]{:S(2)}) collective-permute-start(f32[128,512]{1,0:T(8,128)S(1)} %select_select_fusion.2), channel_id=1, source_target_pairs={{12,60},{76,124},{140,188},{204,252},{13,61},{77,125},{141,189},{2... | collective-permute-start | bytes 786440 | tf_op jit(solution)/shard_map/ppermute | solution.py:72
  111.8 14.3 %collective-permute-start.18 = (f32[128,512]{1,0:T(8,128)S(1)}, f32[128,512]{1,0:T(8,128)S(1)}, u32[]{:S(2)}, u32[]{:S(2)}) collective-permute-start(f32[128,512]{1,0:T(8,128)S(1)} %select_select_fusion), channel_id=1, source_target_pairs={{0,8},{4,12},{8,0},{12,4},{16,24},{20,28},{24,16},{28,20},{32,40},... | collective-permute-start | bytes 786440 | tf_op jit(solution)/shard_map/ppermute | solution.py:79
  126.2 2.2 %collective-permute-start.19 = (f32[128,1024]{1,0:T(8,128)S(1)}, f32[128,1024]{1,0:T(8,128)S(1)}, u32[]{:S(2)}, u32[]{:S(2)}) collective-permute-start(f32[128,1024]{1,0:T(8,128)S(1)} %maximum_select_fusion.1), channel_id=1, source_target_pairs={{0,4},{4,0},{8,12},{12,8},{16,20},{20,16},{24,28},{28,24},{32,36},... | collective-permute-start | bytes 1572872 | tf_op jit(solution)/shard_map/ppermute | solution.py:83
Sparse Core Ops, SparseCore 0:
  66.7 52.6 all-gather.1
